TPU v7x, 128 devices: a whole 4x4x4 slice. The times are simulated.
128 devices in a mesh: freq: 8 (over z_hi, x), blk: 16 (over y, z_lo, core).
Axes of the slice: x: 4, y: 4, z: 4 (z_hi: 2, z_lo: 2; z = z_hi * 2 + z_lo), core: 2. Of those that a mesh axis runs over, the one named last changes fastest.
Arguments:
- traces: bfloat16 [2048, 2048, 256], P('blk', 'freq'), may hold values from -6 to 6
- signature: float32 [8, 2], P('freq'), may hold values from 0.5 to 1.5
Outputs:
- multiples: float32 [8, 2, 2048, 2048], P('freq', None, 'blk')
All inputs are finite; a program needn't handle non-finite values.
Results may differ from a plain program's by a relative error of at most 0.0035.
Values sent between devices are 32-bit elements; how exact they have to be, the bound alone decides.
No kernel may reach another device: no remote copies, remote signals or barrier semaphores. Data moves between devices by JAX's collectives and lax.ppermute only.
A program may use at most 256 MiB of HBM per device.

v0:
```python
import math
import jax
import jax.numpy as jnp
from jax import lax
from jax.sharding import PartitionSpec as P

BIN0 = 4
BINSTEP = 3


def make_table(freqs, samples):
    bins = BIN0 + BINSTEP * jnp.arange(freqs, dtype=jnp.int32)
    steps = jnp.arange(samples, dtype=jnp.int32)
    phase = steps[:, None] * bins[None, :] % samples
    angle = phase.astype(jnp.float32) * (2.0 * math.pi / samples)
    scale = 1.0 / math.sqrt(samples)
    table = jnp.concatenate([jnp.cos(angle) * scale, -jnp.sin(angle) * scale], axis=1)
    return table.astype(jnp.bfloat16)


def complex_dot(a_re, a_im, b_re, b_im):
    hp = lax.Precision.HIGHEST
    real_part = jnp.dot(a_re, b_re, precision=hp) - jnp.dot(a_im, b_im, precision=hp)
    imag_part = jnp.dot(a_re, b_im, precision=hp) + jnp.dot(a_im, b_re, precision=hp)
    return (real_part, imag_part)


def on_device(traces, signature):
    src_rows, rec_cols, samples = traces.shape
    freqs = lax.axis_size("freq")
    table = make_table(freqs, samples)
    projected = jnp.einsum("srt,tc->csr", traces, table, preferred_element_type=jnp.float32)
    projected = projected.reshape(2, freqs, src_rows, rec_cols)
    spectra = lax.all_to_all(projected, "freq", split_axis=1, concat_axis=3, tiled=True)
    own = spectra[:, 0]
    width = own.shape[2]
    own_re = own[0]
    own_im = own[1]
    full = lax.all_gather(own, "blk", axis=1, tiled=True)
    prod_re, prod_im = complex_dot(own_re, own_im, full[0], full[1])
    scale = 1.0 / math.sqrt(width)
    w_re = signature[0, 0]
    w_im = signature[0, 1]
    out_re = -(w_re * prod_re - w_im * prod_im) * scale
    out_im = -(w_re * prod_im + w_im * prod_re) * scale
    return jnp.stack([out_re, out_im], axis=0)[None]


def solution(mesh):
    return jax.shard_map(
        on_device,
        mesh=mesh,
        in_specs=(P("blk", "freq", None), P("freq", None)),
        out_specs=P("freq", None, "blk", None),
        check_vma=False,
    )
```

profile of v0, /device:TPU:1, one launch (start us, length us, event | category | flops | bytes accessed | tf_op | source)
XLA Modules:
  0.0 346.1 jit_solution(8752176337144553729)
XLA Ops:
  6.5 0.0 all-gather.2.cloned.1.call-start
  6.5 0.1 multiply_convert_fusion.1
  6.7 0.0 copy-start.1
  6.7 10.2 %convolution_bitcast_fusion = f32[2,8,128,256]{3,1,0,2:T(8,128)S(1)} fusion(bf16[128,256,256]{2,1,0:T(8,128)(2,1)} %param.2, bf16[256,8]{0,1:T(8,128)(2,1)S(1)} %get-tuple-element.14, bf16[256,8]{0,1:T(8,128)(2,1)S(1)} %get-tuple-element.13), kind=kOutput, calls=%fused_computation.15 | convolution fusion | flops 268451840 | bytes 18882560 | tf_op jit(solution)/shard_map/srt,tc->csr/dot_general | solution.py:32
  16.9 1.1 copy.4
  18.0 36.3 %all_to_all.15 = f32[2,8,128,256]{3,0,2,1:T(2,128)} all-to-all(f32[2,8,128,256]{3,0,2,1:T(2,128)S(1)} %copy.4), channel_id=1, replica_groups=mesh['freq'=8,'blk'=16] {'freq'}, dimensions={1} | all-to-all | bytes 4194304 | tf_op jit(solution)/shard_map/all_to_all | solution.py:34
  54.3 2.7 copy.5
  57.0 2.3 copy.6
  59.4 0.0 all-gather.2.cloned.1.call-update
  59.4 0.0 copy-done.1
  59.4 0.7 fusion.29
  60.1 1.1 fusion.28
  61.2 168.2 %all-gather.2.cloned.1.call-done = f32[2,2048,2048]{2,0,1:T(2,128)} async-done(((f32[2,128,2048]{2,0,1:T(2,128)}), f32[2,2048,2048]{2,0,1:T(2,128)}) %all-gather.2.cloned.1.call-update) | async-done | bytes 33554448 | tf_op jit(solution)/shard_map/all_gather | solution.py:39
  229.4 40.0 %fusion.27 = (f32[1,2048,2048]{2,0,1:T(1,128)}, f32[1,2048,2048]{2,0,1:T(1,128)}) fusion(f32[2,2048,2048]{2,0,1:T(2,128)} %all-gather.2.cloned.1.call-done), kind=kLoop, calls=%fused_computation.34 | loop fusion | bytes 67108864 | tf_op jit(solution)/shard_map/slice | solution.py:40
  269.4 0.0 copy-start
  269.4 0.0 slice-start
  269.4 0.0 slice-start.1
  269.4 18.8 %fusion.2 = f32[128,2048]{1,0:T(8,128)S(1)} fusion(f32[128,2048]{0,1:T(8,128)S(1)} %bitcast.45, f32[1,2048,2048]{2,0,1:T(1,128)} %get-tuple-element.6), kind=kOutput, calls=%fused_computation.2 | convolution fusion | flops 6442450944 | bytes 18874368 | tf_op jit(solution)/shard_map/dot_general | solution.py:23
  288.2 0.0 slice-start.2
  288.2 0.0 copy-done
  288.2 0.0 slice-start.3
  288.2 19.2 %fusion = f32[128,2048]{1,0:T(8,128)S(1)} fusion(f32[128,2048]{0,1:T(8,128)S(1)} %bitcast.47, f32[1,2048,2048]{2,0,1:T(1,128)} %get-tuple-element.6), kind=kOutput, calls=%fused_computation | convolution fusion | flops 6442450944 | bytes 18874368 | tf_op jit(solution)/shard_map/dot_general | solution.py:24
  307.4 0.0 slice-done
  307.5 0.0 slice-done.1
  307.5 0.0 slice-done.2
  307.5 0.0 slice-done.3
  307.5 14.1 %fusion.12 = f32[128,2048]{1,0:T(8,128)S(1)} fusion(f32[128,2048]{1,0:T(8,128)S(1)} %fusion.2, f32[128,2048]{0,1:T(8,128)S(1)} %bitcast.48, f32[1,2048,2048]{2,0,1:T(1,128)S(1)} %bitcast.42), kind=kOutput, calls=%fused_computation.12 | convolution fusion | flops 6442713088 | bytes 19922944 | tf_op jit(solution)/shard_map/dot_general | solution.py:23
  321.6 15.7 %multiply_bitcast_fusion.1 = (f32[1,128,2048]{2,1,0:T(8,128)S(1)}, f32[1,128,2048]{2,1,0:T(8,128)S(1)}) fusion(f32[128,2048]{1,0:T(8,128)S(1)} %fusion.12, f32[]{:T(128)} %bitcast.9, f32[]{:T(128)} %bitcast, f32[128,2048]{1,0:T(8,128)S(1)} %fusion, f32[128,2048]{0,1:T(8,128)S(1)} %bitcast.46, f32[1,2048,2048]{2,0,1:T(1,128)S(1)} %bitcast.42), kind=kOutput, calls=%fused_computation.17 | convolution fusion | flops 6445334528 | bytes 22020104 | tf_op jit(solution)/shard_map/dot_general | solution.py:24
  337.3 1.5 maximum_bitcast_fusion
  (2 shorter events, 0.0 us)
Async XLA Ops:
  6.5 222.8 %all-gather.2.cloned.1.call-start = ((), (), s32[]{:S(2)}) async-start(), calls=%async_computation.1 | async-start | bytes 35651584 | tf_op jit(solution)/shard_map/all_gather | solution.py:39
  6.7 52.7 %copy-start.1 = (f32[1,2]{1,0:T(1,128)S(1)}, f32[1,2]{1,0:T(1,128)}, u32[]{:S(2)}) copy-start(f32[1,2]{1,0:T(1,128)} %param.3) | copy-start | bytes 28
  269.4 18.9 %copy-start = (f32[1,1,128,8,256]{2,4,3,1,0:T(8,128)S(1)}, f32[1,1,128,8,256]{2,4,3,1,0:T(8,128)}, u32[]{:S(2)}) copy-start(f32[1,1,128,8,256]{2,4,3,1,0:T(8,128)} %get-tuple-element.9) | copy-start | bytes 3145732
  269.4 38.1 %slice-start = ((s8[16777216]{0:T(1024)(128)(4,1)}), s8[4194304]{0:T(1024)(128)(4,1)S(1)}, s32[]{:S(2)}) async-start(s8[16777216]{0:T(1024)(128)(4,1)} %bitcast.41), calls=%async_computation.2 | async-start | bytes 8388608
  269.4 38.1 %slice-start.1 = ((s8[16777216]{0:T(1024)(128)(4,1)}), s8[4194304]{0:T(1024)(128)(4,1)S(1)}, s32[]{:S(2)}) async-start(s8[16777216]{0:T(1024)(128)(4,1)} %bitcast.41), calls=%async_computation.3 | async-start | bytes 8388608
  288.2 19.3 %slice-start.2 = ((s8[16777216]{0:T(1024)(128)(4,1)}), s8[4194304]{0:T(1024)(128)(4,1)S(1)}, s32[]{:S(2)}) async-start(s8[16777216]{0:T(1024)(128)(4,1)} %bitcast.41), calls=%async_computation.4 | async-start | bytes 8388608
  288.2 19.3 %slice-start.3 = ((s8[16777216]{0:T(1024)(128)(4,1)}), s8[4194304]{0:T(1024)(128)(4,1)S(1)}, s32[]{:S(2)}) async-start(s8[16777216]{0:T(1024)(128)(4,1)} %bitcast.41), calls=%async_computation.5 | async-start | bytes 8388608
Sparse Core Ops, SparseCore 0:
  59.5 169.8 all-gather.1
where the time goes:
time: 349 us; the launch traced here: 346 us
  waiting for transfers between devices  168 us (48%)
  matrix products  78 us (22%)
  local copies, waits for them, and re-layouts  48 us (14%)
  blocking collectives  36.3 us (10%)
  between operations  14 us (4%)
    all_gather x1, waiting for transfers between devices, on_device(): full = lax.all_gather(own, 'blk', axis=1, tiled=True)  168 us
    slice x1, local copies, waits for them, and re-layouts, on_device(): prod_re, prod_im = complex_dot(own_re, own_im, full[0], full[1])  40 us
    all_to_all x1, blocking collectives, on_device(): lax.all_to_all(projected, 'freq', split_axis=1, concat_axis=3, tiled=True)  36.3 us
    dot_general x1, matrix products, complex_dot(): jnp.dot(a_re, b_im, precision=hp) + jnp.dot(a_im, b_re, precision=hp)  19.2 us
    dot_general x1, matrix products, complex_dot(): jnp.dot(a_im, b_im, precision=hp)  18.8 us
    dot_general x1, matrix products, complex_dot(): jnp.dot(a_im, b_re, precision=hp)  15.7 us
    dot_general x1, matrix products, complex_dot(): jnp.dot(a_re, b_re, precision=hp) - jnp.dot(a_im, b_im, precision=hp)  14.1 us
    dot_general x1, matrix products, on_device(): jnp.einsum('srt,tc->csr', traces, table, preferred_element_type=jnp.float32)  10.2 us
  transfers between devices with their start and end apart: 1, of which 1 were waited for; matrix products, arithmetic and copies ran while one was open for 1% of the time, Pallas kernels for 0%

commit v1 on v0

--- a/solution.py
+++ b/solution.py
@@ -36,7 +36,9 @@
     width = own.shape[2]
     own_re = own[0]
     own_im = own[1]
-    full = lax.all_gather(own, "blk", axis=1, tiled=True)
+    full = jnp.concatenate(
+        lax.all_to_all(jnp.stack([own] * lax.axis_size("blk")), "blk", 0, 0), axis=1
+    )
     prod_re, prod_im = complex_dot(own_re, own_im, full[0], full[1])
     scale = 1.0 / math.sqrt(width)
     w_re = signature[0, 0]

time: 349 us -> 688 us (1.97)
  waiting for transfers between devices: 168 us -> 546 us
  matrix products: 78 us -> 56 us
  between operations: 14 us -> 0.06 us
  local copies, waits for them, and re-layouts: 48 us -> 37.4 us
  starting transfers between devices: 0.01 us -> 7.56 us
    all_to_all x0 -> x1, waiting for transfers between devices: none -> 546 us  [on_device(): lax.all_to_all(jnp.stack([own] * lax.axis_size('blk')), 'blk', 0, 0)]
    all_gather x1 -> x0, waiting for transfers between devices: 168 us -> none  [on_device(): full = lax.all_gather(own, 'blk', axis=1, tiled=True)]
    slice x1, local copies, waits for them, and re-layouts: 40 us -> 17.8 us  [on_device(): prod_re, prod_im = complex_dot(own_re, own_im, full[0], full[1])]
    another operation x0 -> x2, local copies, waits for them, and re-layouts: none -> 14 us  [on_device(): jnp.stack([own] * lax.axis_size('blk'))]
    dot_general x1, matrix products: 19.2 us -> 9.06 us  [complex_dot(): jnp.dot(a_re, b_im, precision=hp) + jnp.dot(a_im, b_re, precision=hp)]
    dot_general x1, matrix products: 18.8 us -> 10.4 us  [complex_dot(): jnp.dot(a_im, b_im, precision=hp)]
    all_to_all x0 -> x1, starting transfers between devices: none -> 7.56 us  [on_device(): lax.all_to_all(jnp.stack([own] * lax.axis_size('blk')), 'blk', 0, 0)]
  transfers between devices with their start and end apart: 1 -> 1, of which waited for: 1 -> 1; matrix products, arithmetic and copies ran while one was open for 1% -> 0% of each run, Pallas kernels for 0% -> 0%
where the time goes in v1:
time: 688 us; the launch traced here: 685 us
  waiting for transfers between devices  546 us (79%)
  matrix products  56 us (8%)
  local copies, waits for them, and re-layouts  37.4 us (5%)
  blocking collectives  35.7 us (5%)
  starting transfers between devices  7.56 us (1%)
    all_to_all x1, waiting for transfers between devices, on_device(): lax.all_to_all(jnp.stack([own] * lax.axis_size('blk')), 'blk', 0, 0)  546 us
    all_to_all x1, blocking collectives, on_device(): lax.all_to_all(projected, 'freq', split_axis=1, concat_axis=3, tiled=True)  35.7 us
    slice x1, local copies, waits for them, and re-layouts, on_device(): prod_re, prod_im = complex_dot(own_re, own_im, full[0], full[1])  17.8 us
    another operation x2, local copies, waits for them, and re-layouts, on_device(): jnp.stack([own] * lax.axis_size('blk'))  14 us
  transfers between devices with their start and end apart: 1, of which 1 were waited for; matrix products, arithmetic and copies ran while one was open for 0% of the time, Pallas kernels for 0%

profile of v1, /device:TPU:1, one launch (start us, length us, event | category | flops | bytes accessed | tf_op | source)
XLA Modules:
  0.0 684.7 jit_solution(11935200161192306992)
XLA Ops:
  0.0 0.1 multiply_convert_fusion.1
  0.1 10.2 %convolution_bitcast_fusion = f32[2,8,128,256]{3,1,0,2:T(8,128)S(1)} fusion(bf16[128,256,256]{2,1,0:T(8,128)(2,1)} %param.2, bf16[256,8]{0,1:T(8,128)(2,1)S(1)} %get-tuple-element.14, bf16[256,8]{0,1:T(8,128)(2,1)S(1)} %get-tuple-element.13), kind=kOutput, calls=%fused_computation.3 | convolution fusion | flops 268451840 | bytes 18882560 | tf_op jit(solution)/shard_map/srt,tc->csr/dot_general | solution.py:32
  10.4 1.1 copy.5
  11.5 35.7 %all_to_all.20 = f32[2,8,128,256]{3,0,2,1:T(2,128)} all-to-all(f32[2,8,128,256]{3,0,2,1:T(2,128)S(1)} %copy.5), channel_id=1, replica_groups=mesh['freq'=8,'blk'=16] {'freq'}, dimensions={1} | all-to-all | bytes 4194304 | tf_op jit(solution)/shard_map/all_to_all | solution.py:34
  47.2 2.7 copy.6
  49.9 1.8 copy.7
  51.7 12.2 %stack.12 = f32[16,2,128,2048]{3,2,1,0:T(8,128)} broadcast(f32[2,128,2048]{2,1,0:T(8,128)} %copy.7), dimensions={1,2,3} | broadcast | bytes 35651584 | tf_op jit(solution)/shard_map/stack | solution.py:40
  63.9 0.0 copy-start.1
  63.9 7.6 %all-to-all-start.1 = ((f32[16,2,128,2048]{3,2,1,0:T(8,128)}), f32[16,2,128,2048]{3,2,1,0:T(8,128)}, u32[]{:S(2)}, u32[]{:S(2)}) async-start(f32[16,2,128,2048]{3,2,1,0:T(8,128)} %stack.12), calls=%async_computation.1 | async-start | bytes 67108864 | tf_op jit(solution)/shard_map/all_to_all | solution.py:40
  71.5 0.0 copy-done.1
  71.5 0.6 fusion.11
  72.1 1.1 fusion.10
  73.2 546.4 %all-to-all-done.1 = f32[16,2,128,2048]{3,2,1,0:T(8,128)} async-done(((f32[16,2,128,2048]{3,2,1,0:T(8,128)}), f32[16,2,128,2048]{3,2,1,0:T(8,128)}, u32[]{:S(2)}, u32[]{:S(2)}) %all-to-all-start.1) | async-done | bytes 33554464 | tf_op jit(solution)/shard_map/all_to_all | solution.py:40
  619.6 0.0 copy-start
  619.6 17.8 %fusion.9 = (f32[1,16,128,2048]{3,2,0,1:T(8,128)S(1)}, f32[1,16,128,2048]{3,2,0,1:T(8,128)}) fusion(f32[2,16,128,2048]{3,2,0,1:T(8,128)} %bitcast.8), kind=kLoop, calls=%fused_computation.22 | loop fusion | bytes 67108864 | tf_op jit(solution)/shard_map/slice | solution.py:42
  637.4 0.0 copy-done
  637.4 9.1 %fusion.13 = f32[128,2048]{1,0:T(8,128)S(1)} fusion(f32[128,2048]{0,1:T(8,128)S(1)} %bitcast.40, f32[2048,2048]{1,0:T(8,128)S(1)} %bitcast.32), kind=kOutput, calls=%fused_computation.26 | convolution fusion | flops 6442450944 | bytes 18874368 | tf_op jit(solution)/shard_map/dot_general | solution.py:24
  646.5 13.3 %fusion.12 = f32[128,2048]{1,0:T(8,128)S(1)} fusion(f32[128,2048]{0,1:T(8,128)S(1)} %bitcast.41, f32[2048,2048]{1,0:T(8,128)} %bitcast.34), kind=kOutput, calls=%fused_computation.25 | convolution fusion | flops 6442450944 | bytes 18874368 | tf_op jit(solution)/shard_map/dot_general | solution.py:23
  659.8 13.0 %convolution_add_fusion = f32[128,2048]{1,0:T(8,128)S(1)} fusion(f32[128,2048]{1,0:T(8,128)S(1)} %fusion.13, f32[128,2048]{0,1:T(8,128)S(1)} %bitcast.38, f32[2048,2048]{1,0:T(8,128)} %bitcast.35), kind=kOutput, calls=%fused_computation | convolution fusion | flops 6442713088 | bytes 19922944 | tf_op jit(solution)/shard_map/dot_general | solution.py:24
  672.8 10.4 %multiply_bitcast_fusion.1 = (f32[1,128,2048]{2,1,0:T(8,128)S(1)}, f32[1,128,2048]{2,1,0:T(8,128)S(1)}) fusion(f32[128,2048]{1,0:T(8,128)S(1)} %convolution_add_fusion, f32[]{:T(128)} %bitcast.12, f32[]{:T(128)} %bitcast, f32[128,2048]{1,0:T(8,128)S(1)} %fusion.12, f32[128,2048]{0,1:T(8,128)S(1)} %bitcast.39, f32[2048,2048]{1,0:T(8,128)S(1)} %bitcast.33), kind=kOutput, calls=%fused_computation.5 | convolution fusion | flops 6445334528 | bytes 22020104 | tf_op jit(solution)/shard_map/dot_general | solution.py:23
  683.2 1.5 maximum_bitcast_fusion
  (1 shorter events, 0.0 us)
Async XLA Ops:
  63.9 7.6 %copy-start.1 = (f32[1,2]{1,0:T(1,128)S(1)}, f32[1,2]{1,0:T(1,128)}, u32[]{:S(2)}) copy-start(f32[1,2]{1,0:T(1,128)} %param.3) | copy-start | bytes 28
  63.9 555.7 %all-to-all-start.1 = ((f32[16,2,128,2048]{3,2,1,0:T(8,128)}), f32[16,2,128,2048]{3,2,1,0:T(8,128)}, u32[]{:S(2)}, u32[]{:S(2)}) async-start(f32[16,2,128,2048]{3,2,1,0:T(8,128)} %stack.12), calls=%async_computation.1 | async-start | bytes 67108864 | tf_op jit(solution)/shard_map/all_to_all | solution.py:40
  619.6 17.8 %copy-start = (f32[1,1,128,8,256]{2,4,3,1,0:T(8,128)S(1)}, f32[1,1,128,8,256]{2,4,3,1,0:T(8,128)}, u32[]{:S(2)}) copy-start(f32[1,1,128,8,256]{2,4,3,1,0:T(8,128)} %get-tuple-element.10) | copy-start | bytes 3145732
